TPU v7x, 32 devices: a whole 2x2x4 slice. The times are simulated.
32 devices in a mesh: groups: 2 (over y), ctx: 4 (over z), mp: 2 (over x), sub: 2 (over core).
Axes of the slice: x: 2, y: 2, z: 4, core: 2. Of those that a mesh axis runs over, the one named last changes fastest.
Arguments:
- features: bfloat16 [16384, 3, 4096], P(('groups', 'ctx'), None, ('mp', 'sub')), parts along dimension 0, may hold values from -6 to 6
- short_filter: float32 [7, 3, 4096], P(None, None, ('mp', 'sub')), may hold values from -2 to 2
- mr_filter: bfloat16 [256, 128], P(('mp', 'sub')), may hold values from -0.5 to 0.5
- lr_gates: bfloat16 [16384, 2, 4096], P(('groups', 'ctx'), None, ('mp', 'sub')), parts along dimension 0, may hold values from -6 to 6
- lr_rate: float32 [4096, 16], P(('mp', 'sub')), may hold values from 6.1035156e-05 to 0.05
- lr_residue: float32 [4096, 16], P(('mp', 'sub')), may hold values from -2 to 2
- lr_skip: float32 [4096], P(('mp', 'sub')), may hold values from -3 to 3
Outputs:
- output: bfloat16 [16384, 4096], P(('groups', 'ctx'), ('mp', 'sub')), parts along dimension 0
There are 2 independent parts, one for each index of `groups`. A program takes and returns all parts, laid end to end along the dimension named above; an argument that names none is the same for every part. Nothing has to cross between parts.
All inputs are finite; a program needn't handle non-finite values.
Results may differ from a plain program's by a relative error of at most 0.0059.
Values may be sent and summed in bfloat16 or wider, within the bound.
No kernel may reach another device: no remote copies, remote signals or barrier semaphores. Data moves between devices by JAX's collectives and lax.ppermute only.
A program may use at most 192 MiB of HBM per device.

v0:
```python
import jax
import jax.numpy as jnp
from jax import lax
from jax.sharding import PartitionSpec as P

TAPS = 128
SHORT = 7


def passed_along(shard, axis, by):
    devices = lax.axis_size(axis)
    pairs = [(i, i + by) for i in range(devices) if 0 <= i + by < devices]
    return lax.ppermute(shard, axis, pairs)


def featurize(extended, weights):
    width = weights.shape[0]
    count = extended.shape[0] - (width - 1)
    total = jnp.zeros((count,) + extended.shape[1:], jnp.float32)
    for j in range(width):
        total = total + weights[j] * extended[width - 1 - j : width - 1 - j + count]
    return total


def medium_mix(extended, filters):
    groups, taps = filters.shape
    rows = extended.shape[0] - (taps - 1)
    chans = extended.shape[1]
    padded = jnp.concatenate([jnp.zeros((1, chans), jnp.bfloat16), extended], 0)
    blocks = rows // taps
    before = padded[:rows].reshape(blocks, taps, chans)
    current = padded[taps:].reshape(blocks, taps, chans)
    window = jnp.concatenate([before, current], 1).reshape(
        blocks, 2 * taps, groups, chans // groups
    )
    window = window.transpose(2, 3, 0, 1)
    lag = jnp.arange(taps)[:, None] + taps - jnp.arange(2 * taps)[None, :]
    valid = (lag >= 0) & (lag < taps)
    toeplitz = jnp.where(
        valid[None], filters[:, jnp.clip(lag, 0, taps - 1)], jnp.zeros((), jnp.bfloat16)
    )
    mixed = jnp.einsum("gts,gkbs->gkbt", toeplitz, window, preferred_element_type=jnp.float32)
    return mixed.transpose(2, 3, 0, 1).reshape(rows, chans)


def modal_local(signal, rate_modes, residue_modes):
    rows_block = 64
    count, chans = signal.shape
    blocks = count // rows_block
    weight = residue_modes * jnp.sqrt(rate_modes)
    steps = jnp.arange(rows_block).astype(jnp.float32)
    decay_in = jnp.exp(-rate_modes[None] * steps[:, None, None])
    kernel = jnp.einsum("trc,rc->tc", decay_in, weight, precision=lax.Precision.HIGHEST)
    lag = jnp.arange(rows_block)[:, None] - jnp.arange(rows_block)[None, :]
    toeplitz = jnp.where((lag >= 0)[:, :, None], kernel[jnp.maximum(lag, 0)], 0.0)
    blocked = signal.astype(jnp.float32).reshape(blocks, rows_block, chans)
    intra = jnp.einsum("tsc,bsc->btc", toeplitz, blocked, precision=lax.Precision.HIGHEST)
    decay_out = jnp.exp(-rate_modes[None] * (rows_block - 1 - steps)[:, None, None])
    contrib = jnp.einsum("bsc,src->brc", blocked, decay_out, precision=lax.Precision.HIGHEST)
    gap = (jnp.arange(blocks)[:, None] - jnp.arange(blocks)[None, :] - 1).astype(jnp.float32)
    before_mask = gap >= 0.0
    gap_rows = jnp.maximum(gap, 0.0) * rows_block

    def mode_prefix(pair):
        rate_one, contrib_one = pair
        decay = jnp.where(
            before_mask[:, :, None], jnp.exp(-rate_one[None, None, :] * gap_rows[:, :, None]), 0.0
        )
        return jnp.einsum("xbc,bc->xc", decay, contrib_one, precision=lax.Precision.HIGHEST)

    incoming = lax.map(mode_prefix, (rate_modes, contrib.transpose(1, 0, 2))).transpose(1, 0, 2)
    last_state = incoming[-1] * jnp.exp(-rate_modes * rows_block) + contrib[-1]
    readout = jnp.exp(-rate_modes[None] * (steps + 1.0)[:, None, None]) * weight[None]
    return (intra, incoming, last_state, readout)


def modal_finish(intra, incoming, readout):
    state = jnp.einsum("brc,trc->btc", incoming, readout, precision=lax.Precision.HIGHEST)
    return (intra + state).reshape(-1, intra.shape[2])


def per_device(features, short_filter, mr_filter, lr_gates, lr_rate, lr_residue, lr_skip):
    count = features.shape[0]
    rim = passed_along(features[count - (SHORT - 1) :], "ctx", 1)
    featured = featurize(jnp.concatenate([rim, features], 0), short_filter)
    query = featured[:, 0]
    product = (featured[:, 1] * featured[:, 2]).astype(jnp.bfloat16)
    prior = passed_along(product[count - (TAPS - 1) :], "ctx", 1)
    extended = jnp.concatenate([prior, product], 0)
    mixed = medium_mix(extended, mr_filter)
    lr_input = (lr_gates[:, 1] * query * mixed).astype(jnp.bfloat16)
    spread = lax.all_to_all(lr_input, "ctx", split_axis=1, concat_axis=0, tiled=True)
    width = spread.shape[1]
    offset = lax.axis_index("ctx") * width
    rate_modes = lax.dynamic_slice_in_dim(lr_rate, offset, width, 0).T
    residue_modes = lax.dynamic_slice_in_dim(lr_residue, offset, width, 0).T
    intra, incoming, last_state, readout = modal_local(spread, rate_modes, residue_modes)
    part_mix = modal_finish(intra, incoming, readout)
    long_mix = lax.all_to_all(part_mix, "ctx", split_axis=0, concat_axis=1, tiled=True)
    return (lr_gates[:, 0] * (long_mix + lr_skip * lr_input.astype(jnp.float32))).astype(
        jnp.bfloat16
    )


def solution(mesh):
    in_specs = (
        P(("groups", "ctx"), None, ("mp", "sub")),
        P(None, None, ("mp", "sub")),
        P(("mp", "sub"), None),
        P(("groups", "ctx"), None, ("mp", "sub")),
        P(("mp", "sub"), None),
        P(("mp", "sub"), None),
        P(("mp", "sub")),
    )
    out_specs = P(("groups", "ctx"), ("mp", "sub"))
    return jax.shard_map(
        per_device, mesh=mesh, in_specs=in_specs, out_specs=out_specs, check_vma=False
    )
```

profile of v0, /device:TPU:0, one launch (start us, length us, event | category | flops | bytes accessed | tf_op | source)
XLA Modules:
  0.0 906.1 jit_solution(622854457128697138)
XLA Ops:
  7.3 17.8 %fusion.47 = (bf16[2048,1,1024]{2,1,0:T(2,128)(2,1)}, bf16[2048,1,1024]{2,1,0:T(2,128)(2,1)}) fusion(bf16[2048,2,1024]{2,1,0:T(2,128)(2,1)} %param.12), kind=kLoop, calls=%fused_computation.89 | loop fusion | bytes 16777216 | tf_op jit(solution)/shard_map/slice | solution.py:100
  25.2 16.9 %copy.54 = bf16[2048,3,1024]{0,2,1:T(8,128)(2,1)} copy(bf16[2048,3,1024]{2,0,1:T(8,128)(2,1)} %param.9) | data formatting | bytes 25165824 | tf_op args[0]
  42.1 19.8 %copy.94 = bf16[2048,1,1024]{0,2,1:T(8,128)(2,1)} copy(bf16[2048,1,1024]{2,1,0:T(2,128)(2,1)} %get-tuple-element.70) | data formatting | bytes 8388608
  62.5 66.6 %multiply_add_fusion = f32[2048,3,1024]{0,2,1:T(8,128)} fusion(bf16[2048,3,1024]{0,2,1:T(8,128)(2,1)} %copy.54, bf16[6,3,1024]{0,2,1:T(8,128)(2,1)S(1)} %copy.55, f32[3,1024]{1,0:T(4,128)S(1)} %get-tuple-element.78, f32[3,1024]{1,0:T(4,128)S(1)} %get-tuple-element.79, f32[3,1024]{1,0:T(4,128)S(1)} %get-tuple-element.80, f32[3,1024]{1,0:T(4,128)S(1)} %get-tuple-element.81, ...), kind=kLoop, calls=%fused_computation.15 | loop fusion | flops 239075328 | bytes 37871616 | tf_op jit(solution)/shard_map/add | solution.py:21
  129.1 14.6 %fusion.10 = (bf16[2048,1,1024]{0,2,1:T(8,128)(2,1)S(1)}, f32[2048,1,1024]{0,2,1:T(8,128)}) fusion(f32[2048,3,1024]{0,2,1:T(8,128)} %multiply_add_fusion, bf16[2048,1,1024]{0,2,1:T(8,128)(2,1)} %copy.94), kind=kLoop, calls=%fused_computation.28 | loop fusion | flops 8388608 | bytes 41943040 | tf_op jit(solution)/shard_map/convert_element_type | solution.py:87
  147.7 114.9 %gather_fusion = bf16[32768,64]{1,0:T(8,128)(2,1)} fusion(bf16[64,128]{0,1:T(8,128)(2,1)S(1)} %copy.57, s32[32768]{0:T(1024)S(1)} %broadcast_clamp_fusion), kind=kCustom, calls=%fused_computation | custom fusion | bytes 8519680 | tf_op jit(solution)/shard_map/gather | solution.py:40
  262.6 10.1 %copy.58 = bf16[128,256,64]{1,0,2:T(8,128)(2,1)} copy(bf16[128,256,64]{2,1,0:T(8,128)(2,1)} %bitcast.122) | data formatting | bytes 8388608 | tf_op jit(solution)/shard_map/gather | solution.py:40
  300.3 9.3 %reshape.164 = f32[2048,4,256]{0,2,1:T(8,128)} reshape(f32[16,128,64,16]{1,0,3,2:T(8,128)} %bitcast.119) | data formatting | bytes 16777216 | tf_op jit(solution)/shard_map/reshape | solution.py:43
  309.6 9.2 %multiply_convert_fusion = bf16[2048,4,256]{0,2,1:T(8,128)(2,1)} fusion(f32[2048,4,256]{0,2,1:T(8,128)} %bitcast.116, f32[2048,4,256]{0,2,1:T(8,128)} %reshape.164), kind=kLoop, calls=%fused_computation.40 | loop fusion | flops 4194304 | bytes 20971520 | tf_op jit(solution)/shard_map/convert_element_type | solution.py:91
  326.8 16.1 %gather_fusion.1 = f32[4096,256]{1,0:T(8,128)} fusion(f32[64,256]{1,0:T(8,128)S(1)} %bitcast.115, s32[4096]{0:T(1024)S(1)} %broadcast_clamp_fusion.1), kind=kCustom, calls=%fused_computation.1 | custom fusion | bytes 8404992 | tf_op jit(solution)/shard_map/gather | solution.py:55
  342.9 9.2 %copy.61 = f32[64,64,256]{1,0,2:T(8,128)} copy(f32[64,64,256]{2,1,0:T(8,128)} %bitcast.124) | data formatting | bytes 8388608 | tf_op jit(solution)/shard_map/gather | solution.py:55
  352.1 64.5 %all-to-all-done = bf16[2048,4,256]{0,2,1:T(8,128)(2,1)} async-done(((bf16[2048,4,256]{0,2,1:T(8,128)(2,1)}), bf16[2048,4,256]{0,2,1:T(8,128)(2,1)}, u32[]{:S(2)}, u32[]{:S(2)}) %all-to-all-start) | async-done | bytes 4194336 | tf_op jit(solution)/shard_map/all_to_all | solution.py:92
  435.4 215.4 %while.11 = (s32[]{:T(128)}, f32[16,128,256]{1,0,2:T(8,128)}, f32[16,128,256]{1,0,2:T(8,128)S(1)}, f32[16,256]{1,0:T(8,128)S(1)}, s32[]{:T(128)}, /*index=5*/s32[]{:T(128)}) while((s32[]{:T(128)}, f32[16,128,256]{1,0,2:T(8,128)}, f32[16,128,256]{1,0,2:T(8,128)S(1)}, f32[16,256]{1,0:T(8,128)S(1)}, s32[]{:T(128)}, ...), condition=%wide.region_1.2_spmd.clone, body=%wide.region_0.1_spmd.clone.sunk | while | flops 16892160 | bytes 1477713 | solution.py:71
  435.7 8.4 multiply_reduce_fusion.3
  449.2 8.4 multiply_reduce_fusion.3
  462.6 8.4 multiply_reduce_fusion.3
  476.1 8.4 multiply_reduce_fusion.3
  650.8 17.9 %fusion.28 = f32[256,64,128]{2,1,0:T(8,128)} fusion(f32[16,128,256]{1,0,2:T(8,128)} %get-tuple-element.37, f32[16,256]{0,1:T(8,128)S(1)} %copy.63, f32[64]{0:T(128)S(1)} %broadcast_add_fusion, f32[16,256]{0,1:T(8,128)S(1)} %copy.60), kind=kOutput, calls=%fused_computation.52 | convolution fusion | flops 403177472 | bytes 10518784 | tf_op jit(solution)/shard_map/brc,trc->btc/dot_general | solution.py:78
  668.7 10.5 %bitcast_add_fusion.1 = f32[128,64,256]{0,1,2:T(8,128)} fusion(f32[256,64,128]{2,1,0:T(8,128)} %fusion.28, bf16[128,64,256]{0,1,2:T(8,128)(2,1)S(1)} %copy-done.1, f32[64,64,256]{1,0,2:T(8,128)} %copy.61, pred[64,64]{1,0:T(8,128)(4,1)S(1)} %subtract_compare_fusion), kind=kOutput, calls=%fused_computation.37 | convolution fusion | flops 1613758464 | bytes 25169920 | tf_op jit(solution)/shard_map/tsc,bsc->btc/dot_general | solution.py:57
  679.2 9.2 %copy.67 = f32[128,64,256]{2,1,0:T(8,128)} copy(f32[128,64,256]{0,1,2:T(8,128)} %bitcast_add_fusion.1) | data formatting | bytes 16777216 | tf_op jit(solution)/shard_map/add | solution.py:79
  694.4 19.9 %copy.95 = bf16[2048,1,1024]{0,2,1:T(8,128)(2,1)} copy(bf16[2048,1,1024]{2,1,0:T(2,128)(2,1)} %get-tuple-element.69) | data formatting | bytes 8388608
  714.2 162.5 %all-to-all-done.1 = f32[4,2048,256]{2,1,0:T(8,128)} async-done(((f32[4,2048,256]{2,1,0:T(8,128)}), f32[4,2048,256]{2,1,0:T(8,128)}, u32[]{:S(2)}, u32[]{:S(2)}) %all-to-all-start.1) | async-done | bytes 8388640 | tf_op jit(solution)/shard_map/all_to_all | solution.py:99
  876.7 8.7 copy.68
  885.4 14.3 %fusion.14 = bf16[2048,1024]{0,1:T(8,128)(2,1)} fusion(f32[2048,4,256]{0,2,1:T(8,128)} %copy.68, f32[128,8,16,128]{3,2,1,0:T(8,128)} %bitcast.120, f32[2048,1,1024]{0,2,1:T(8,128)} %get-tuple-element.68, bf16[2048,1,1024]{0,2,1:T(8,128)(2,1)} %copy.95, f32[1024]{0:T(1024)S(1)} %copy-done.5), kind=kLoop, calls=%fused_computation.35 | loop fusion | flops 16777216 | bytes 33558528 | tf_op jit(solution)/shard_map/convert_element_type | solution.py:100
  (181 shorter events, 259.6 us)
Async XLA Ops:
  0.8 61.3 %collective-permute-start = (bf16[6,3,1024]{2,0,1:T(8,128)(2,1)S(1)}, bf16[6,3,1024]{2,0,1:T(8,128)(2,1)S(1)}, u32[]{:S(2)}, u32[]{:S(2)}) collective-permute-start(bf16[6,3,1024]{2,0,1:T(8,128)(2,1)S(1)} %slice.70), channel_id=1, source_target_pairs={{0,4},{4,8},{8,12},{1,5},{5,9},{9,13},{2,6},{6,10},{10,14},{3,7},{... | collective-permute-start | bytes 110600 | tf_op jit(solution)/shard_map/ppermute | solution.py:13
  129.1 18.5 %copy-start.4 = (bf16[64,128]{1,0:T(8,128)(2,1)S(1)}, bf16[64,128]{1,0:T(8,128)(2,1)}, u32[]{:S(2)}) copy-start(bf16[64,128]{1,0:T(8,128)(2,1)} %param.11) | copy-start | bytes 49156
  143.7 3.8 copy-start
  143.9 134.6 %collective-permute-start.1 = (bf16[127,1024]{0,1:T(8,128)(2,1)S(1)}, bf16[127,1024]{0,1:T(8,128)(2,1)S(1)}, u32[]{:S(2)}, u32[]{:S(2)}) collective-permute-start(bf16[127,1024]{0,1:T(8,128)(2,1)S(1)} %slice_bitcast_fusion.1), channel_id=1, source_target_pairs={{0,4},{4,8},{8,12},{1,5},{5,9},{9,13},{2,6},{6,10},{10,14},{3,7},{... | collective-permute-start | bytes 780296 | tf_op jit(solution)/shard_map/ppermute | solution.py:13
  286.5 6.1 copy-start.2
  286.5 6.1 copy-start.3
  318.8 97.8 %all-to-all-start = ((bf16[2048,4,256]{0,2,1:T(8,128)(2,1)}), bf16[2048,4,256]{0,2,1:T(8,128)(2,1)}, u32[]{:S(2)}, u32[]{:S(2)}) async-start(bf16[2048,4,256]{0,2,1:T(8,128)(2,1)} %multiply_convert_fusion), calls=%async_computation | async-start | bytes 8388608 | tf_op jit(solution)/shard_map/all_to_all | solution.py:92
  650.8 17.9 %copy-start.1 = (bf16[128,64,256]{0,1,2:T(8,128)(2,1)S(1)}, bf16[128,64,256]{0,1,2:T(8,128)(2,1)}, u32[]{:S(2)}) copy-start(bf16[128,64,256]{0,1,2:T(8,128)(2,1)} %copy.62) | copy-start | bytes 12582916
  688.4 188.3 %all-to-all-start.1 = ((f32[4,2048,256]{2,1,0:T(8,128)}), f32[4,2048,256]{2,1,0:T(8,128)}, u32[]{:S(2)}, u32[]{:S(2)}) async-start(f32[4,2048,256]{2,1,0:T(8,128)} %bitcast.121), calls=%async_computation.1 | async-start | bytes 16777216 | tf_op jit(solution)/shard_map/all_to_all | solution.py:99
  876.7 8.7 copy-start.5
where the time goes:
time: 910 us; the launch traced here: 906 us
  local copies, waits for them, and re-layouts  374 us (41%)
  other arithmetic  243 us (27%)
  waiting for transfers between devices  227 us (25%)
  matrix products  41.4 us (5%)
  starting transfers between devices  19.7 us (2%)
    all_to_all x1, waiting for transfers between devices, per_device(): lax.all_to_all(part_mix, 'ctx', split_axis=0, concat_axis=1, tiled=True)  162 us
    dot_general x16, other arithmetic, mode_prefix(): jnp.einsum('xbc,bc->xc', decay, contrib_one, precision=lax.Precision.HIGH...  134 us
    gather x2, local copies, waits for them, and re-layouts, medium_mix(): filters[:, jnp.clip(lag, 0, taps - 1)]  125 us
    dynamic_update_slice x32, local copies, waits for them, and re-layouts, modal_local(): lax.map(mode_prefix, (rate_modes, contrib.transpose(1, 0, 2)))  76.3 us
    unnamed x25, local copies, waits for them, and re-layouts  68.7 us
    add x1, other arithmetic, featurize(): total = total + weights[j] * extended[width - 1 - j:width - 1 - j + count]  66.6 us
    all_to_all x1, waiting for transfers between devices, per_device(): lax.all_to_all(lr_input, 'ctx', split_axis=1, concat_axis=0, tiled=True)  64.5 us
    gather x2, local copies, waits for them, and re-layouts, modal_local(): kernel[jnp.maximum(lag, 0)]  25.3 us
  transfers between devices with their start and end apart: 4, of which 2 were waited for; matrix products, arithmetic and copies ran while one was open for 26% of the time, Pallas kernels for 0%

commit v1 on v0

--- a/solution.py
+++ b/solution.py
@@ -5,6 +5,18 @@
 
 TAPS = 128
 SHORT = 7
+
+
+def in_blocks(x, dim, count):
+    shape = x.shape
+    blocks = x.reshape(*shape[:dim], count, shape[dim] // count, *shape[dim + 1 :])
+    return jnp.moveaxis(blocks, dim, 0)
+
+
+def laid_out(blocks, dim):
+    shape = list(blocks.shape[1:])
+    shape[dim] *= blocks.shape[0]
+    return jnp.moveaxis(blocks, 0, dim).reshape(shape)
 
 
 def passed_along(shard, axis, by):
@@ -89,7 +101,17 @@
     extended = jnp.concatenate([prior, product], 0)
     mixed = medium_mix(extended, mr_filter)
     lr_input = (lr_gates[:, 1] * query * mixed).astype(jnp.bfloat16)
-    spread = lax.all_to_all(lr_input, "ctx", split_axis=1, concat_axis=0, tiled=True)
+    size, index = (lax.axis_size("ctx"), lax.axis_index("ctx"))
+    parts = in_blocks(lr_input, 1, size)
+    out = parts
+    for hop in range(1, size):
+        target, source = ((index + hop) % size, (index - hop) % size)
+        sent = lax.dynamic_index_in_dim(parts, target, 0)
+        partner_block = lax.ppermute(
+            sent, "ctx", [(i_2, (i_2 + hop) % size) for i_2 in range(size)]
+        )
+        out = lax.dynamic_update_slice_in_dim(out, partner_block, source, axis=0)
+    spread = laid_out(out, 0)
     width = spread.shape[1]
     offset = lax.axis_index("ctx") * width
     rate_modes = lax.dynamic_slice_in_dim(lr_rate, offset, width, 0).T

time: 910 us -> 916 us (level)
  waiting for transfers between devices: 227 us -> 201 us
  starting transfers between devices: 19.7 us -> 37.5 us
  local copies, waits for them, and re-layouts: 374 us -> 384 us
    all_to_all x1 -> x0, waiting for transfers between devices: 64.5 us -> none  [per_device(): lax.all_to_all(lr_input, 'ctx', split_axis=1, concat_axis=0, tiled=True)]
    ppermute x0 -> x3, waiting for transfers between devices: none -> 37.7 us  [per_device(): lax.ppermute(sent, 'ctx', [(i_2, (i_2 + hop) % size) for i_2 in range(siz...]
    all_to_all x1, starting transfers between devices: 5.94 us -> 24.2 us  [per_device(): lax.all_to_all(part_mix, 'ctx', split_axis=0, concat_axis=1, tiled=True)]
    dynamic_update_slice x0 -> x4, local copies, waits for them, and re-layouts: none -> 10.6 us  [per_device(): out = lax.dynamic_update_slice_in_dim(out, partner_block, source, axis=0)]
    unnamed x25 -> x27, local copies, waits for them, and re-layouts: 68.7 us -> 72.9 us
  transfers between devices with their start and end apart: 4 -> 6, of which waited for: 2 -> 2; matrix products, arithmetic and copies ran while one was open for 26% -> 26% of each run, Pallas kernels for 0% -> 0%
where the time goes in v1:
time: 916 us; the launch traced here: 906 us
  local copies, waits for them, and re-layouts  384 us (42%)
  other arithmetic  241 us (26%)
  waiting for transfers between devices  201 us (22%)
  matrix products  41.6 us (5%)
  starting transfers between devices  37.5 us (4%)
    all_to_all x1, waiting for transfers between devices, per_device(): lax.all_to_all(part_mix, 'ctx', split_axis=0, concat_axis=1, tiled=True)  164 us
    dot_general x16, other arithmetic, mode_prefix(): jnp.einsum('xbc,bc->xc', decay, contrib_one, precision=lax.Precision.HIGH...  134 us
    gather x2, local copies, waits for them, and re-layouts, medium_mix(): filters[:, jnp.clip(lag, 0, taps - 1)]  124 us
    dynamic_update_slice x32, local copies, waits for them, and re-layouts, modal_local(): lax.map(mode_prefix, (rate_modes, contrib.transpose(1, 0, 2)))  76.2 us
    unnamed x27, local copies, waits for them, and re-layouts  72.9 us
    add x1, other arithmetic, featurize(): total = total + weights[j] * extended[width - 1 - j:width - 1 - j + count]  66.5 us
    ppermute x3, waiting for transfers between devices, per_device(): lax.ppermute(sent, 'ctx', [(i_2, (i_2 + hop) % size) for i_2 in range(siz...  37.7 us
    gather x2, local copies, waits for them, and re-layouts, modal_local(): kernel[jnp.maximum(lag, 0)]  25.2 us
  transfers between devices with their start and end apart: 6, of which 2 were waited for; matrix products, arithmetic and copies ran while one was open for 26% of the time, Pallas kernels for 0%

profile of v1, /device:TPU:0, one launch (start us, length us, event | category | flops | bytes accessed | tf_op | source)
XLA Modules:
  0.0 906.3 jit_solution(11276994769572805772)
XLA Ops:
  7.3 17.8 %fusion.47 = (bf16[2048,1,1024]{2,1,0:T(2,128)(2,1)}, bf16[2048,1,1024]{2,1,0:T(2,128)(2,1)}) fusion(bf16[2048,2,1024]{2,1,0:T(2,128)(2,1)} %param.12), kind=kLoop, calls=%fused_computation.95 | loop fusion | bytes 16777216 | tf_op jit(solution)/shard_map/slice | solution.py:122
  25.2 17.1 %copy.54 = bf16[2048,3,1024]{0,2,1:T(8,128)(2,1)} copy(bf16[2048,3,1024]{2,0,1:T(8,128)(2,1)} %param.9) | data formatting | bytes 25165824 | tf_op args[0]
  42.4 19.8 %copy.94 = bf16[2048,1,1024]{0,2,1:T(8,128)(2,1)} copy(bf16[2048,1,1024]{2,1,0:T(2,128)(2,1)} %get-tuple-element.70) | data formatting | bytes 8388608
  62.7 66.5 %multiply_add_fusion = f32[2048,3,1024]{0,2,1:T(8,128)} fusion(bf16[2048,3,1024]{0,2,1:T(8,128)(2,1)} %copy.54, bf16[6,3,1024]{0,2,1:T(8,128)(2,1)S(1)} %copy.55, f32[3,1024]{1,0:T(4,128)S(1)} %get-tuple-element.81, f32[3,1024]{1,0:T(4,128)S(1)} %get-tuple-element.82, f32[3,1024]{1,0:T(4,128)S(1)} %get-tuple-element.83, f32[3,1024]{1,0:T(4,128)S(1)} %get-tuple-element.84, ...), kind=kLoop, calls=%fused_computation.15 | loop fusion | flops 239075328 | bytes 37871616 | tf_op jit(solution)/shard_map/add | solution.py:33
  129.3 14.7 %fusion.10 = (bf16[2048,1,1024]{0,2,1:T(8,128)(2,1)S(1)}, f32[2048,1,1024]{0,2,1:T(8,128)}) fusion(f32[2048,3,1024]{0,2,1:T(8,128)} %multiply_add_fusion, bf16[2048,1,1024]{0,2,1:T(8,128)(2,1)} %copy.94), kind=kLoop, calls=%fused_computation.28 | loop fusion | flops 8388608 | bytes 41943040 | tf_op jit(solution)/shard_map/convert_element_type | solution.py:99
  150.1 114.2 %gather_fusion = bf16[32768,64]{1,0:T(8,128)(2,1)} fusion(bf16[64,128]{0,1:T(8,128)(2,1)S(1)} %copy.57, s32[32768]{0:T(1024)S(1)} %broadcast_clamp_fusion), kind=kCustom, calls=%fused_computation | custom fusion | bytes 8519680 | tf_op jit(solution)/shard_map/gather | solution.py:52
  264.3 10.1 %copy.58 = bf16[128,256,64]{1,0,2:T(8,128)(2,1)} copy(bf16[128,256,64]{2,1,0:T(8,128)(2,1)} %bitcast.129) | data formatting | bytes 8388608 | tf_op jit(solution)/shard_map/gather | solution.py:52
  302.0 9.3 %reshape.166 = f32[2048,4,256]{0,2,1:T(8,128)} reshape(f32[16,128,64,16]{1,0,3,2:T(8,128)} %bitcast.125) | data formatting | bytes 16777216 | tf_op jit(solution)/shard_map/reshape | solution.py:55
  329.7 16.1 %gather_fusion.1 = f32[4096,256]{1,0:T(8,128)} fusion(f32[64,256]{1,0:T(8,128)S(1)} %bitcast.121, s32[4096]{0:T(1024)S(1)} %broadcast_clamp_fusion.1), kind=kCustom, calls=%fused_computation.1 | custom fusion | bytes 8404992 | tf_op jit(solution)/shard_map/gather | solution.py:67
  345.7 9.1 %copy.61 = f32[64,64,256]{1,0,2:T(8,128)} copy(f32[64,64,256]{2,1,0:T(8,128)} %bitcast.131) | data formatting | bytes 8388608 | tf_op jit(solution)/shard_map/gather | solution.py:67
  355.9 37.7 %collective-permute-done.3 = bf16[1,2048,256]{1,2,0:T(8,128)(2,1)S(1)} collective-permute-done((bf16[1,2048,256]{1,2,0:T(8,128)(2,1)}, bf16[1,2048,256]{1,2,0:T(8,128)(2,1)S(1)}, u32[]{:S(2)}, u32[]{:S(2)}) %collective-permute-start.3) | collective-permute-done | bytes 1048608 | tf_op jit(solution)/shard_map/ppermute | solution.py:110
  415.8 215.3 %while.11 = (s32[]{:T(128)}, f32[16,128,256]{1,0,2:T(8,128)}, f32[16,128,256]{1,0,2:T(8,128)S(1)}, f32[16,256]{1,0:T(8,128)S(1)}, s32[]{:T(128)}, /*index=5*/s32[]{:T(128)}) while((s32[]{:T(128)}, f32[16,128,256]{1,0,2:T(8,128)}, f32[16,128,256]{1,0,2:T(8,128)S(1)}, f32[16,256]{1,0:T(8,128)S(1)}, s32[]{:T(128)}, ...), condition=%wide.region_1.2_spmd.clone, body=%wide.region_0.1_spmd.clone.sunk | while | flops 16892160 | bytes 1477713 | solution.py:83
  443.0 8.4 multiply_reduce_fusion.3
  456.4 8.4 multiply_reduce_fusion.3
  469.9 8.4 multiply_reduce_fusion.3
  483.3 8.4 multiply_reduce_fusion.3
  631.1 18.0 %fusion.28 = f32[256,64,128]{2,1,0:T(8,128)} fusion(f32[16,128,256]{1,0,2:T(8,128)} %get-tuple-element.37, f32[16,256]{0,1:T(8,128)S(1)} %copy.63, f32[64]{0:T(128)S(1)} %broadcast_add_fusion, f32[16,256]{0,1:T(8,128)S(1)} %copy.60), kind=kOutput, calls=%fused_computation.52 | convolution fusion | flops 403177472 | bytes 10518784 | tf_op jit(solution)/shard_map/brc,trc->btc/dot_general | solution.py:90
  649.1 10.5 %bitcast_add_fusion.1 = f32[128,64,256]{0,1,2:T(8,128)} fusion(f32[256,64,128]{2,1,0:T(8,128)} %fusion.28, bf16[128,64,256]{0,1,2:T(8,128)(2,1)S(1)} %copy-done.1, f32[64,64,256]{1,0,2:T(8,128)} %copy.61, pred[64,64]{1,0:T(8,128)(4,1)S(1)} %subtract_compare_fusion), kind=kOutput, calls=%fused_computation.37 | convolution fusion | flops 1613758464 | bytes 25169920 | tf_op jit(solution)/shard_map/tsc,bsc->btc/dot_general | solution.py:69
  659.6 9.2 %copy.67 = f32[128,64,256]{2,1,0:T(8,128)} copy(f32[128,64,256]{0,1,2:T(8,128)} %bitcast_add_fusion.1) | data formatting | bytes 16777216 | tf_op jit(solution)/shard_map/add | solution.py:91
  668.9 24.2 %all-to-all-start = ((f32[4,2048,256]{2,1,0:T(8,128)}), f32[4,2048,256]{2,1,0:T(8,128)}, u32[]{:S(2)}, u32[]{:S(2)}) async-start(f32[4,2048,256]{2,1,0:T(8,128)} %bitcast.127), calls=%async_computation | async-start | bytes 16777216 | tf_op jit(solution)/shard_map/all_to_all | solution.py:121
  693.1 19.9 %copy.95 = bf16[2048,1,1024]{0,2,1:T(8,128)(2,1)} copy(bf16[2048,1,1024]{2,1,0:T(2,128)(2,1)} %get-tuple-element.69) | data formatting | bytes 8388608
  713.0 163.7 %all-to-all-done = f32[4,2048,256]{2,1,0:T(8,128)} async-done(((f32[4,2048,256]{2,1,0:T(8,128)}), f32[4,2048,256]{2,1,0:T(8,128)}, u32[]{:S(2)}, u32[]{:S(2)}) %all-to-all-start) | async-done | bytes 8388640 | tf_op jit(solution)/shard_map/all_to_all | solution.py:121
  876.6 8.7 copy.68
  885.4 14.3 %fusion.14 = bf16[2048,1024]{0,1:T(8,128)(2,1)} fusion(f32[2048,4,256]{0,2,1:T(8,128)} %copy.68, f32[128,8,16,128]{3,2,1,0:T(8,128)} %bitcast.126, f32[2048,1,1024]{0,2,1:T(8,128)} %get-tuple-element.68, bf16[2048,1,1024]{0,2,1:T(8,128)(2,1)} %copy.95, f32[1024]{0:T(1024)S(1)} %copy-done.6), kind=kLoop, calls=%fused_computation.35 | loop fusion | flops 16777216 | bytes 33558528 | tf_op jit(solution)/shard_map/convert_element_type | solution.py:122
  (191 shorter events, 270.3 us)
Async XLA Ops:
  0.8 61.5 %collective-permute-start = (bf16[6,3,1024]{2,0,1:T(8,128)(2,1)S(1)}, bf16[6,3,1024]{2,0,1:T(8,128)(2,1)S(1)}, u32[]{:S(2)}, u32[]{:S(2)}) collective-permute-start(bf16[6,3,1024]{2,0,1:T(8,128)(2,1)S(1)} %slice.70), channel_id=1, source_target_pairs={{0,4},{4,8},{8,12},{1,5},{5,9},{9,13},{2,6},{6,10},{10,14},{3,7},{... | collective-permute-start | bytes 110600 | tf_op jit(solution)/shard_map/ppermute | solution.py:25
  129.3 20.7 %copy-start.5 = (bf16[64,128]{1,0:T(8,128)(2,1)S(1)}, bf16[64,128]{1,0:T(8,128)(2,1)}, u32[]{:S(2)}) copy-start(bf16[64,128]{1,0:T(8,128)(2,1)} %param.11) | copy-start | bytes 49156
  143.9 2.0 copy-start
  146.1 134.0 %collective-permute-start.1 = (bf16[127,1024]{0,1:T(8,128)(2,1)S(1)}, bf16[127,1024]{0,1:T(8,128)(2,1)S(1)}, u32[]{:S(2)}, u32[]{:S(2)}) collective-permute-start(bf16[127,1024]{0,1:T(8,128)(2,1)S(1)} %slice_bitcast_fusion.1), channel_id=1, source_target_pairs={{0,4},{4,8},{8,12},{1,5},{5,9},{9,13},{2,6},{6,10},{10,14},{3,7},{... | collective-permute-start | bytes 780296 | tf_op jit(solution)/shard_map/ppermute | solution.py:25
  288.1 6.1 copy-start.3
  288.1 6.1 copy-start.4
  318.4 2.0 copy-start.2
  322.2 32.6 %collective-permute-start.2 = (bf16[1,2048,256]{1,2,0:T(8,128)(2,1)}, bf16[1,2048,256]{1,2,0:T(8,128)(2,1)S(1)}, u32[]{:S(2)}, u32[]{:S(2)}) collective-permute-start(bf16[1,2048,256]{1,2,0:T(8,128)(2,1)} %get-tuple-element.73), channel_id=1, source_target_pairs={{0,4},{4,8},{8,12},{12,0},{1,5},{5,9},{9,13},{13,1},{2,6},{6,10},{... | collective-permute-start | bytes 3145736 | tf_op jit(solution)/shard_map/ppermute | solution.py:110
  324.9 68.7 %collective-permute-start.3 = (bf16[1,2048,256]{1,2,0:T(8,128)(2,1)}, bf16[1,2048,256]{1,2,0:T(8,128)(2,1)S(1)}, u32[]{:S(2)}, u32[]{:S(2)}) collective-permute-start(bf16[1,2048,256]{1,2,0:T(8,128)(2,1)} %get-tuple-element.72), channel_id=1, source_target_pairs={{0,8},{4,12},{8,0},{12,4},{1,9},{5,13},{9,1},{13,5},{2,10},{6,14},... | collective-permute-start | bytes 3145736 | tf_op jit(solution)/shard_map/ppermute | solution.py:110
  326.8 67.9 %collective-permute-start.4 = (bf16[1,2048,256]{1,2,0:T(8,128)(2,1)}, bf16[1,2048,256]{1,2,0:T(8,128)(2,1)}, u32[]{:S(2)}, u32[]{:S(2)}) collective-permute-start(bf16[1,2048,256]{1,2,0:T(8,128)(2,1)} %get-tuple-element.71), channel_id=1, source_target_pairs={{0,12},{4,0},{8,4},{12,8},{1,13},{5,1},{9,5},{13,9},{2,14},{6,2},{... | collective-permute-start | bytes 3145736 | tf_op jit(solution)/shard_map/ppermute | solution.py:110
  631.0 18.1 %copy-start.1 = (bf16[128,64,256]{0,1,2:T(8,128)(2,1)S(1)}, bf16[128,64,256]{0,1,2:T(8,128)(2,1)}, u32[]{:S(2)}) copy-start(bf16[128,64,256]{0,1,2:T(8,128)(2,1)} %copy.62) | copy-start | bytes 12582916
  668.9 207.8 %all-to-all-start = ((f32[4,2048,256]{2,1,0:T(8,128)}), f32[4,2048,256]{2,1,0:T(8,128)}, u32[]{:S(2)}, u32[]{:S(2)}) async-start(f32[4,2048,256]{2,1,0:T(8,128)} %bitcast.127), calls=%async_computation | async-start | bytes 16777216 | tf_op jit(solution)/shard_map/all_to_all | solution.py:121
  876.6 8.7 copy-start.6
